TPU v7x, 256 devices: a whole 4x4x8 slice. The times are simulated.
256 devices in a mesh: rep: 32 (over z, y_hi, core), fsdp: 8 (over x, y_lo).
Axes of the slice: x: 4, y: 4 (y_hi: 2, y_lo: 2; y = y_hi * 2 + y_lo), z: 8, core: 2. Of those that a mesh axis runs over, the one named last changes fastest.
Arguments:
- hidden: bfloat16 [32768, 7168], P(('rep', 'fsdp')), may hold values from -6 to 6
- grad_out: bfloat16 [32768, 4096], P(('rep', 'fsdp')), may hold values from -24 to 24
- down_weight: bfloat16 [7168, 4096], P('fsdp'), may hold values from -0.0625 to 0.0625
- hash_tiles: bfloat16 [3, 32, 7168], P(None, None, 'fsdp'), may hold values from -1 to 1, as said below
- momentum: float32 [8, 3, 32, 4096], P('fsdp', None, None, 'rep'), may hold values from -6 to 6
- error: float32 [8, 3, 32, 4096], P('fsdp', None, None, 'rep'), may hold values from -6 to 6
Outputs:
- grad_hidden: bfloat16 [32768, 7168], P(('rep', 'fsdp'))
- update: float32 [7168, 4096], P('fsdp', 'rep')
- new_momentum: float32 [8, 3, 32, 4096], P('fsdp', None, None, 'rep')
- new_error: float32 [8, 3, 32, 4096], P('fsdp', None, None, 'rep')
Inputs may be any that keep to these rules, and one draw needn't show every extreme that they name: `hash_tiles`: in every sketch row each hidden unit has exactly one nonzero entry, +1 or -1, in one of the 32 buckets; all other entries are 0.
All inputs are finite; a program needn't handle non-finite values.
Results may differ from a plain program's by a relative error of at most 0.0005.
Values may be sent and summed in bfloat16 or wider, within the bound.
No kernel may reach another device: no remote copies, remote signals or barrier semaphores. Data moves between devices by JAX's collectives and lax.ppermute only.
A program may use at most 128 MiB of HBM per device.

v0:
```python
import math
import jax
import jax.numpy as jnp
from jax import lax
from jax.sharding import PartitionSpec as P

momentum_decay = 0.9
step_size = 0.5


def split3(x):
    hi = lax.reduce_precision(x, exponent_bits=8, mantissa_bits=7)
    r1 = x - hi
    mid = lax.reduce_precision(r1, exponent_bits=8, mantissa_bits=7)
    lo = r1 - mid
    return jnp.stack([hi, mid, lo]).astype(jnp.bfloat16)


def grouped_scatter(blocks):
    me = lax.axis_index("rep")
    replicas = blocks.shape[0]
    inner = 4
    outer = replicas // inner
    rest = blocks.shape[1:]
    data = blocks.reshape((outer, inner) + rest)
    low = me % inner
    kept = lax.dynamic_index_in_dim(data, low, axis=1, keepdims=False)
    for mask in range(1, inner):
        send = lax.dynamic_index_in_dim(data, low ^ mask, axis=1, keepdims=False)
        kept = kept + lax.ppermute(send, "rep", [(j, j ^ mask) for j in range(replicas)])
    high = me // inner
    total = lax.dynamic_index_in_dim(kept, high, axis=0, keepdims=False)
    for mask in range(1, outer):
        send = lax.dynamic_index_in_dim(kept, high ^ mask, axis=0, keepdims=False)
        total = total + lax.ppermute(send, "rep", [(j, j ^ mask * inner) for j in range(replicas)])
    return total[None]


def on_device(hidden, grad_out, down_weight, hash_tiles, momentum, error):
    shards = lax.axis_size("fsdp")
    replicas = lax.axis_size("rep")
    tok_rows = grad_out.shape[0]
    model_width = grad_out.shape[1]
    shard_rows = down_weight.shape[0]
    rows_count = hash_tiles.shape[0]
    buckets = hash_tiles.shape[1]
    sketch_rows = rows_count * buckets
    columns = model_width // replicas
    total_tokens = tok_rows * shards * replicas
    table_scale = math.sqrt(buckets / (shard_rows * total_tokens))
    hash_float = hash_tiles.astype(jnp.float32)
    outgoing = jnp.concatenate(
        [
            jnp.broadcast_to(grad_out[None], (shards, tok_rows, model_width)),
            hidden.reshape(tok_rows, shards, shard_rows).transpose(1, 0, 2),
        ],
        axis=2,
    )
    arrived = lax.all_to_all(outgoing, "fsdp", split_axis=0, concat_axis=0, tiled=True)
    gathered = arrived[:, :, :model_width]
    hidden_cols = arrived[:, :, model_width:]
    partial_grads = jnp.einsum(
        "ptd,hd->tph", gathered, down_weight, preferred_element_type=jnp.float32
    ).astype(jnp.bfloat16)
    grad_hidden = lax.all_to_all(
        partial_grads, "fsdp", split_axis=1, concat_axis=1, tiled=True
    ).reshape(tok_rows, shards * shard_rows)
    projected = jnp.einsum(
        "ki,pti->kpt",
        hash_tiles.reshape(sketch_rows, shard_rows),
        hidden_cols,
        preferred_element_type=jnp.float32,
    ).reshape(sketch_rows, shards * tok_rows)
    pieces = split3(projected).reshape(3 * sketch_rows, shards * tok_rows)
    products = jnp.einsum(
        "mpt,ptd->md",
        pieces.reshape(3 * sketch_rows, shards, tok_rows),
        gathered,
        preferred_element_type=jnp.float32,
    ).reshape(3, sketch_rows, replicas, columns)
    summed = (products[0] + products[1] + products[2]).transpose(1, 0, 2)
    sketch_table = grouped_scatter(
        (summed * table_scale).reshape(replicas, rows_count, buckets, columns)
    )
    new_momentum = momentum_decay * momentum + sketch_table
    accumulated = error + step_size * new_momentum
    update = (
        jnp.einsum("jbi,jbc->ic", hash_float, accumulated[0], precision=lax.Precision.HIGHEST)
        / rows_count
    )
    encoded = jnp.einsum("jbi,ic->jbc", hash_float, update, precision=lax.Precision.HIGHEST)
    new_error = accumulated - encoded[None]
    return (grad_hidden, update, new_momentum, new_error)


def solution(mesh):
    return jax.shard_map(
        on_device,
        mesh=mesh,
        in_specs=(
            P(("rep", "fsdp"), None),
            P(("rep", "fsdp"), None),
            P("fsdp", None),
            P(None, None, "fsdp"),
            P("fsdp", None, None, "rep"),
            P("fsdp", None, None, "rep"),
        ),
        out_specs=(
            P(("rep", "fsdp"), None),
            P("fsdp", "rep"),
            P("fsdp", None, None, "rep"),
            P("fsdp", None, None, "rep"),
        ),
        check_vma=False,
    )
```

profile of v0, /device:TPU:1, one launch (start us, length us, event | category | flops | bytes accessed | tf_op | source)
XLA Modules:
  0.0 227.3 jit_solution(13042546810772492705)
XLA Ops:
  0.6 0.0 copy-start
  0.7 4.0 %copy.15 = bf16[128,7168]{0,1:T(8,128)(2,1)} copy(bf16[128,7168]{1,0:T(8,128)(2,1)} %param.6) | data formatting | bytes 3670016 | tf_op args[0]
  4.6 3.1 %copy.16 = bf16[128,8,896]{2,0,1:T(8,128)(2,1)S(1)} copy(bf16[128,8,896]{0,2,1:T(8,128)(2,1)} %bitcast.97) | data formatting | bytes 3670016 | tf_op jit(solution)/shard_map/reshape | solution.py:55
  7.7 1.0 broadcast_in_dim.12
  8.7 6.8 %pad_maximum_fusion = bf16[8,128,4992]{2,1,0:T(8,128)(2,1)} fusion(bf16[8,128,896]{2,1,0:T(8,128)(2,1)S(1)} %bitcast.95, bf16[8,128,4096]{2,1,0:T(8,128)(2,1)S(1)} %broadcast_in_dim.12), kind=kLoop, calls=%fused_computation | loop fusion | flops 20447232 | bytes 20447232 | tf_op jit(solution)/shard_map/concatenate | solution.py:52
  15.5 5.9 %all-to-all-start = ((bf16[8,128,4992]{2,1,0:T(8,128)(2,1)}), bf16[8,128,4992]{2,1,0:T(8,128)(2,1)}, u32[]{:S(2)}, u32[]{:S(2)}) async-start(bf16[8,128,4992]{2,1,0:T(8,128)(2,1)} %pad_maximum_fusion), calls=%async_computation | async-start | bytes 20447232 | tf_op jit(solution)/shard_map/all_to_all | solution.py:59
  21.4 139.0 %all-to-all-done = bf16[8,128,4992]{2,1,0:T(8,128)(2,1)} async-done(((bf16[8,128,4992]{2,1,0:T(8,128)(2,1)}), bf16[8,128,4992]{2,1,0:T(8,128)(2,1)}, u32[]{:S(2)}, u32[]{:S(2)}) %all-to-all-start) | async-done | bytes 10223648 | tf_op jit(solution)/shard_map/all_to_all | solution.py:59
  160.4 2.2 fusion.17
  162.5 0.2 copy.18
  162.8 0.1 reshape.73
  162.9 0.1 reduce-precision_convert_fusion.1
  163.0 0.1 pad_maximum_fusion.1
  163.0 0.1 copy.26
  163.1 5.0 %fusion.5 = f32[288,4096]{1,0:T(8,128)S(1)} fusion(bf16[8,128,4992]{2,1,0:T(8,128)(2,1)} %all-to-all-done, bf16[288,8,128]{2,1,0:T(8,128)(2,1)S(1)} %bitcast.101), kind=kOutput, calls=%fused_computation.6 | convolution fusion | flops 2415919104 | bytes 13697024 | tf_op jit(solution)/shard_map/mpt,ptd->md/dot_general | solution.py:75
  168.2 0.0 slice-start
  168.2 0.3 fusion.15
  168.5 0.0 slice-start.1
  168.5 0.3 copy.27
  168.7 1.8 constant_dynamic-slice_fusion.3
  170.5 0.1 copy.34
  170.6 5.3 %collective-permute-start.2 = (f32[8,3,32,128]{3,2,1,0:T(8,128)S(1)}, f32[8,3,32,128]{3,2,1,0:T(8,128)}, u32[]{:S(2)}, u32[]{:S(2)}) collective-permute-start(f32[8,3,32,128]{3,2,1,0:T(8,128)S(1)} %bitcast.102), channel_id=1, source_target_pairs={{0,24},{8,16},{16,8},{24,0},{32,56},{40,48},{48,40},{56,32},{64,88... | collective-permute-start | bytes 1179656 | tf_op jit(solution)/shard_map/ppermute | solution.py:30
  175.9 0.1 copy.35
  175.9 0.1 collective-permute-start.1
  176.1 0.8 copy.36
  176.9 0.4 collective-permute-start
  177.3 12.2 %convert_bitcast_fusion = bf16[128,8,896]{2,0,1:T(8,128)(2,1)} fusion(bf16[896,4096]{1,0:T(8,128)(2,1)S(1)} %bitcast.105, bf16[8,128,4992]{2,1,0:T(8,128)(2,1)} %all-to-all-done), kind=kOutput, calls=%fused_computation.9 | convolution fusion | flops 7517110272 | bytes 17563648 | tf_op jit(solution)/shard_map/ptd,hd->tph/dot_general | solution.py:62
  189.5 3.7 %all-to-all-start.1 = ((bf16[128,8,896]{2,0,1:T(8,128)(2,1)}), bf16[128,8,896]{2,0,1:T(8,128)(2,1)S(1)}, u32[]{:S(2)}, u32[]{:S(2)}) async-start(bf16[128,8,896]{2,0,1:T(8,128)(2,1)} %convert_bitcast_fusion), calls=%async_computation.1 | async-start | bytes 3670016 | tf_op jit(solution)/shard_map/all_to_all | solution.py:65
  193.3 0.5 collective-permute-done.1
  193.8 0.0 collective-permute-done
  193.8 1.4 fusion.25
  195.3 5.7 %collective-permute-start.9 = (f32[3,32,128]{2,1,0:T(8,128)S(1)}, f32[3,32,128]{2,1,0:T(8,128)S(1)}, u32[]{:S(2)}, u32[]{:S(2)}) collective-permute-start(f32[3,32,128]{2,1,0:T(8,128)S(1)} %get-tuple-element.17), channel_id=1, source_target_pairs={{0,224},{8,232},{16,240},{24,248},{32,192},{40,200},{48,208},{56,2... | collective-permute-start | bytes 147464 | tf_op jit(solution)/shard_map/ppermute | solution.py:35
  201.0 0.6 collective-permute-start.8
  201.5 3.5 %collective-permute-start.7 = (f32[3,32,128]{2,1,0:T(8,128)S(1)}, f32[3,32,128]{2,1,0:T(8,128)S(1)}, u32[]{:S(2)}, u32[]{:S(2)}) collective-permute-start(f32[3,32,128]{2,1,0:T(8,128)S(1)} %get-tuple-element.19), channel_id=1, source_target_pairs={{0,160},{8,168},{16,176},{24,184},{32,128},{40,136},{48,144},{56,1... | collective-permute-start | bytes 147464 | tf_op jit(solution)/shard_map/ppermute | solution.py:35
  205.0 1.8 collective-permute-start.6
  206.8 1.6 collective-permute-start.5
  208.4 0.0 collective-permute-done.9
  208.4 0.0 collective-permute-start.4
  208.5 1.9 collective-permute-start.3
  210.4 2.0 collective-permute-done.6
  212.4 0.0 collective-permute-done.5
  212.4 3.6 %collective-permute-done.4 = f32[3,32,128]{2,1,0:T(8,128)S(1)} collective-permute-done((f32[3,32,128]{2,1,0:T(8,128)S(1)}, f32[3,32,128]{2,1,0:T(8,128)S(1)}, u32[]{:S(2)}, u32[]{:S(2)}) %collective-permute-start.4) | collective-permute-done | bytes 49184 | tf_op jit(solution)/shard_map/ppermute | solution.py:35
  216.0 0.0 copy-start.2
  216.1 0.4 fusion.16
  216.5 1.0 copy.25
  217.4 1.0 fusion.20
  218.5 2.6 %all-to-all-done.1 = bf16[128,8,896]{2,0,1:T(8,128)(2,1)S(1)} async-done(((bf16[128,8,896]{2,0,1:T(8,128)(2,1)}), bf16[128,8,896]{2,0,1:T(8,128)(2,1)S(1)}, u32[]{:S(2)}, u32[]{:S(2)}) %all-to-all-start.1) | async-done | bytes 1835040 | tf_op jit(solution)/shard_map/all_to_all | solution.py:65
  221.1 2.4 %copy.17 = bf16[128,8,896]{0,2,1:T(8,128)(2,1)} copy(bf16[128,8,896]{2,0,1:T(8,128)(2,1)S(1)} %all-to-all-done.1) | data formatting | bytes 3670016 | tf_op jit(solution)/shard_map/all_to_all | solution.py:65
  223.5 3.9 %copy.24 = bf16[128,7168]{1,0:T(8,128)(2,1)} copy(bf16[128,7168]{0,1:T(8,128)(2,1)} %bitcast.96) | data formatting | bytes 3670016
  (17 shorter events, 0.1 us)
Async XLA Ops:
  0.6 159.7 %copy-start = (bf16[3,32,896]{2,1,0:T(8,128)(2,1)S(1)}, bf16[3,32,896]{2,1,0:T(8,128)(2,1)}, u32[]{:S(2)}) copy-start(bf16[3,32,896]{2,1,0:T(8,128)(2,1)} %param.9) | copy-start | bytes 516100
  0.6 7.0 %copy-start.1 = (bf16[128,4096]{1,0:T(8,128)(2,1)S(1)}, bf16[128,4096]{1,0:T(8,128)(2,1)}, u32[]{:S(2)}) copy-start(bf16[128,4096]{1,0:T(8,128)(2,1)} %param.7) | copy-start | bytes 3145732
  15.5 144.8 %all-to-all-start = ((bf16[8,128,4992]{2,1,0:T(8,128)(2,1)}), bf16[8,128,4992]{2,1,0:T(8,128)(2,1)}, u32[]{:S(2)}, u32[]{:S(2)}) async-start(bf16[8,128,4992]{2,1,0:T(8,128)(2,1)} %pad_maximum_fusion), calls=%async_computation | async-start | bytes 20447232 | tf_op jit(solution)/shard_map/all_to_all | solution.py:59
  168.2 9.1 %slice-start = ((s8[7340032]{0:T(1024)(128)(4,1)}), s8[4194304]{0:T(1024)(128)(4,1)S(1)}, s32[]{:S(2)}) async-start(s8[7340032]{0:T(1024)(128)(4,1)} %bitcast.104), calls=%async_computation.2 | async-start | bytes 8388608
  168.5 8.8 %slice-start.1 = ((s8[7340032]{0:T(1024)(128)(4,1)}), s8[3145728]{0:T(1024)(128)(4,1)S(1)}, s32[]{:S(2)}) async-start(s8[7340032]{0:T(1024)(128)(4,1)} %bitcast.104), calls=%async_computation.3 | async-start | bytes 6291456
  170.6 22.7 %collective-permute-start.2 = (f32[8,3,32,128]{3,2,1,0:T(8,128)S(1)}, f32[8,3,32,128]{3,2,1,0:T(8,128)}, u32[]{:S(2)}, u32[]{:S(2)}) collective-permute-start(f32[8,3,32,128]{3,2,1,0:T(8,128)S(1)} %bitcast.102), channel_id=1, source_target_pairs={{0,24},{8,16},{16,8},{24,0},{32,56},{40,48},{48,40},{56,32},{64,88... | collective-permute-start | bytes 1179656 | tf_op jit(solution)/shard_map/ppermute | solution.py:30
  175.9 17.9 %collective-permute-start.1 = (f32[8,3,32,128]{3,2,1,0:T(8,128)S(1)}, f32[8,3,32,128]{3,2,1,0:T(8,128)}, u32[]{:S(2)}, u32[]{:S(2)}) collective-permute-start(f32[8,3,32,128]{3,2,1,0:T(8,128)S(1)} %bitcast.103), channel_id=1, source_target_pairs={{0,16},{8,24},{16,0},{24,8},{32,48},{40,56},{48,32},{56,40},{64,80... | collective-permute-start | bytes 1179656 | tf_op jit(solution)/shard_map/ppermute | solution.py:30
  176.9 16.9 %collective-permute-start = (f32[8,3,32,128]{3,2,1,0:T(8,128)}, f32[8,3,32,128]{3,2,1,0:T(8,128)}, u32[]{:S(2)}, u32[]{:S(2)}) collective-permute-start(f32[8,3,32,128]{3,2,1,0:T(8,128)} %bitcast.93), channel_id=1, source_target_pairs={{0,8},{8,0},{16,24},{24,16},{32,40},{40,32},{48,56},{56,48},{64,72... | collective-permute-start | bytes 1179656 | tf_op jit(solution)/shard_map/ppermute | solution.py:30
  189.5 26.5 %copy-start.4 = (f32[1,3,32,128]{3,2,1,0:T(8,128)S(1)}, f32[1,3,32,128]{3,2,1,0:T(8,128)}, u32[]{:S(2)}) copy-start(f32[1,3,32,128]{3,2,1,0:T(8,128)} %param.10) | copy-start | bytes 147460
  189.5 26.6 %copy-start.3 = (f32[1,3,32,128]{3,2,1,0:T(8,128)S(1)}, f32[1,3,32,128]{3,2,1,0:T(8,128)}, u32[]{:S(2)}) copy-start(f32[1,3,32,128]{3,2,1,0:T(8,128)} %param.11) | copy-start | bytes 147460
  189.5 31.6 %all-to-all-start.1 = ((bf16[128,8,896]{2,0,1:T(8,128)(2,1)}), bf16[128,8,896]{2,0,1:T(8,128)(2,1)S(1)}, u32[]{:S(2)}, u32[]{:S(2)}) async-start(bf16[128,8,896]{2,0,1:T(8,128)(2,1)} %convert_bitcast_fusion), calls=%async_computation.1 | async-start | bytes 3670016 | tf_op jit(solution)/shard_map/all_to_all | solution.py:65
  195.3 13.2 %collective-permute-start.9 = (f32[3,32,128]{2,1,0:T(8,128)S(1)}, f32[3,32,128]{2,1,0:T(8,128)S(1)}, u32[]{:S(2)}, u32[]{:S(2)}) collective-permute-start(f32[3,32,128]{2,1,0:T(8,128)S(1)} %get-tuple-element.17), channel_id=1, source_target_pairs={{0,224},{8,232},{16,240},{24,248},{32,192},{40,200},{48,208},{56,2... | collective-permute-start | bytes 147464 | tf_op jit(solution)/shard_map/ppermute | solution.py:35
  201.0 7.5 %collective-permute-start.8 = (f32[3,32,128]{2,1,0:T(8,128)S(1)}, f32[3,32,128]{2,1,0:T(8,128)S(1)}, u32[]{:S(2)}, u32[]{:S(2)}) collective-permute-start(f32[3,32,128]{2,1,0:T(8,128)S(1)} %get-tuple-element.18), channel_id=1, source_target_pairs={{0,192},{8,200},{16,208},{24,216},{32,224},{40,232},{48,240},{56,2... | collective-permute-start | bytes 147464 | tf_op jit(solution)/shard_map/ppermute | solution.py:35
  201.5 8.8 %collective-permute-start.7 = (f32[3,32,128]{2,1,0:T(8,128)S(1)}, f32[3,32,128]{2,1,0:T(8,128)S(1)}, u32[]{:S(2)}, u32[]{:S(2)}) collective-permute-start(f32[3,32,128]{2,1,0:T(8,128)S(1)} %get-tuple-element.19), channel_id=1, source_target_pairs={{0,160},{8,168},{16,176},{24,184},{32,128},{40,136},{48,144},{56,1... | collective-permute-start | bytes 147464 | tf_op jit(solution)/shard_map/ppermute | solution.py:35
  205.0 7.4 %collective-permute-start.6 = (f32[3,32,128]{2,1,0:T(8,128)S(1)}, f32[3,32,128]{2,1,0:T(8,128)S(1)}, u32[]{:S(2)}, u32[]{:S(2)}) collective-permute-start(f32[3,32,128]{2,1,0:T(8,128)S(1)} %get-tuple-element.20), channel_id=1, source_target_pairs={{0,128},{8,136},{16,144},{24,152},{32,160},{40,168},{48,176},{56,1... | collective-permute-start | bytes 147464 | tf_op jit(solution)/shard_map/ppermute | solution.py:35
  206.8 5.6 %collective-permute-start.5 = (f32[3,32,128]{2,1,0:T(8,128)S(1)}, f32[3,32,128]{2,1,0:T(8,128)S(1)}, u32[]{:S(2)}, u32[]{:S(2)}) collective-permute-start(f32[3,32,128]{2,1,0:T(8,128)S(1)} %get-tuple-element.21), channel_id=1, source_target_pairs={{0,96},{8,104},{16,112},{24,120},{32,64},{40,72},{48,80},{56,88},{... | collective-permute-start | bytes 147464 | tf_op jit(solution)/shard_map/ppermute | solution.py:35
  208.4 7.5 %collective-permute-start.4 = (f32[3,32,128]{2,1,0:T(8,128)S(1)}, f32[3,32,128]{2,1,0:T(8,128)S(1)}, u32[]{:S(2)}, u32[]{:S(2)}) collective-permute-start(f32[3,32,128]{2,1,0:T(8,128)S(1)} %get-tuple-element.22), channel_id=1, source_target_pairs={{0,64},{8,72},{16,80},{24,88},{32,96},{40,104},{48,112},{56,120},{... | collective-permute-start | bytes 147464 | tf_op jit(solution)/shard_map/ppermute | solution.py:35
  208.5 7.5 %collective-permute-start.3 = (f32[3,32,128]{2,1,0:T(8,128)S(1)}, f32[3,32,128]{2,1,0:T(8,128)S(1)}, u32[]{:S(2)}, u32[]{:S(2)}) collective-permute-start(f32[3,32,128]{2,1,0:T(8,128)S(1)} %get-tuple-element.16), channel_id=1, source_target_pairs={{0,32},{8,40},{16,48},{24,56},{32,0},{40,8},{48,16},{56,24},{64,96... | collective-permute-start | bytes 147464 | tf_op jit(solution)/shard_map/ppermute | solution.py:35
  216.0 11.3 %copy-start.2 = (f32[1,3,32,128]{3,2,1,0:T(8,128)}, f32[1,3,32,128]{3,2,1,0:T(8,128)S(1)}, u32[]{:S(2)}) copy-start(f32[1,3,32,128]{3,2,1,0:T(8,128)S(1)} %bitcast_add_fusion.1) | copy-start | bytes 147460
where the time goes:
time: 228 us; the launch traced here: 227 us
  waiting for transfers between devices  148 us (65%)
  starting transfers between devices  30.4 us (13%)
  matrix products  20.8 us (9%)
  local copies, waits for them, and re-layouts  18.8 us (8%)
  other arithmetic  8.67 us (4%)
    all_to_all x1, waiting for transfers between devices, on_device(): lax.all_to_all(outgoing, 'fsdp', split_axis=0, concat_axis=0, tiled=True)  139 us
    ppermute x7, starting transfers between devices, grouped_scatter(): lax.ppermute(send, 'rep', [(j, j ^ mask * inner) for j in range(replicas)])  15.1 us
    dot_general x1, matrix products, on_device(): jnp.einsum('ptd,hd->tph', gathered, down_weight, preferred_element_type=j...  12.2 us
    unnamed x19, local copies, waits for them, and re-layouts  9.23 us
    concatenate x1, other arithmetic, on_device(): jnp.concatenate([jnp.broadcast_to(grad_out[None], (shards, tok_rows, mode...  6.79 us
    all_to_all x1, starting transfers between devices, on_device(): lax.all_to_all(outgoing, 'fsdp', split_axis=0, concat_axis=0, tiled=True)  5.86 us
    ppermute x3, starting transfers between devices, grouped_scatter(): lax.ppermute(send, 'rep', [(j, j ^ mask) for j in range(replicas)])  5.76 us
    ppermute x7, waiting for transfers between devices, grouped_scatter(): lax.ppermute(send, 'rep', [(j, j ^ mask * inner) for j in range(replicas)])  5.62 us
  transfers between devices with their start and end apart: 12, of which 5 were waited for; matrix products, arithmetic and copies ran while one was open for 7% of the time, Pallas kernels for 0%

commit v1 on v0

--- a/solution.py
+++ b/solution.py
@@ -6,6 +6,12 @@
 
 momentum_decay = 0.9
 step_size = 0.5
+
+
+def swap_blocks(x, name, split, join):
+    pieces = jnp.split(x, lax.axis_size(name), axis=split)
+    received = lax.all_to_all(jnp.stack(pieces), name, 0, 0)
+    return jnp.concatenate(received, axis=join)
 
 
 def split3(x):
@@ -62,9 +68,7 @@
     partial_grads = jnp.einsum(
         "ptd,hd->tph", gathered, down_weight, preferred_element_type=jnp.float32
     ).astype(jnp.bfloat16)
-    grad_hidden = lax.all_to_all(
-        partial_grads, "fsdp", split_axis=1, concat_axis=1, tiled=True
-    ).reshape(tok_rows, shards * shard_rows)
+    grad_hidden = swap_blocks(partial_grads, "fsdp", 1, 1).reshape(tok_rows, shards * shard_rows)
     projected = jnp.einsum(
         "ki,pti->kpt",
         hash_tiles.reshape(sketch_rows, shard_rows),

time: 228 us -> 258 us (1.13)
  waiting for transfers between devices: 148 us -> 171 us
  local copies, waits for them, and re-layouts: 18.8 us -> 24.4 us
    ppermute x3, waiting for transfers between devices: 0.54 us -> 26.9 us  [grouped_scatter(): lax.ppermute(send, 'rep', [(j, j ^ mask) for j in range(replicas)])]
    unnamed x19 -> x22, local copies, waits for them, and re-layouts: 9.23 us -> 14.1 us
  transfers between devices with their start and end apart: 12 -> 12, of which waited for: 5 -> 5; matrix products, arithmetic and copies ran while one was open for 7% -> 2% of each run, Pallas kernels for 0% -> 0%
where the time goes in v1:
time: 258 us; the launch traced here: 257 us
  waiting for transfers between devices  171 us (66%)
  starting transfers between devices  30.4 us (12%)
  local copies, waits for them, and re-layouts  24.4 us (9%)
  matrix products  22.1 us (9%)
  other arithmetic  8.81 us (3%)
    all_to_all x1, waiting for transfers between devices, on_device(): lax.all_to_all(outgoing, 'fsdp', split_axis=0, concat_axis=0, tiled=True)  139 us
    ppermute x3, waiting for transfers between devices, grouped_scatter(): lax.ppermute(send, 'rep', [(j, j ^ mask) for j in range(replicas)])  26.9 us
    ppermute x7, starting transfers between devices, grouped_scatter(): lax.ppermute(send, 'rep', [(j, j ^ mask * inner) for j in range(replicas)])  15.1 us
    unnamed x22, local copies, waits for them, and re-layouts  14.1 us
    dot_general x1, matrix products, on_device(): jnp.einsum('ptd,hd->tph', gathered, down_weight, preferred_element_type=j...  13.4 us
    concatenate x1, other arithmetic, on_device(): jnp.concatenate([jnp.broadcast_to(grad_out[None], (shards, tok_rows, mode...  6.93 us
    all_to_all x1, starting transfers between devices, on_device(): lax.all_to_all(outgoing, 'fsdp', split_axis=0, concat_axis=0, tiled=True)  5.86 us
    ppermute x3, starting transfers between devices, grouped_scatter(): lax.ppermute(send, 'rep', [(j, j ^ mask) for j in range(replicas)])  5.82 us
  transfers between devices with their start and end apart: 12, of which 5 were waited for; matrix products, arithmetic and copies ran while one was open for 2% of the time, Pallas kernels for 0%

profile of v1, /device:TPU:1, one launch (start us, length us, event | category | flops | bytes accessed | tf_op | source)
XLA Modules:
  0.0 257.4 jit_solution(14614801623805323550)
XLA Ops:
  0.6 3.9 %copy.15 = bf16[128,7168]{0,1:T(8,128)(2,1)} copy(bf16[128,7168]{1,0:T(8,128)(2,1)} %param.6) | data formatting | bytes 3670016 | tf_op args[0]
  4.6 3.1 %copy.16 = bf16[128,8,896]{2,0,1:T(8,128)(2,1)S(1)} copy(bf16[128,8,896]{0,2,1:T(8,128)(2,1)} %bitcast.131) | data formatting | bytes 3670016 | tf_op jit(solution)/shard_map/reshape | solution.py:61
  7.7 1.0 broadcast_in_dim.12
  8.8 6.9 %pad_maximum_fusion = bf16[8,128,4992]{2,1,0:T(8,128)(2,1)} fusion(bf16[8,128,896]{2,1,0:T(8,128)(2,1)S(1)} %bitcast.128, bf16[8,128,4096]{2,1,0:T(8,128)(2,1)S(1)} %broadcast_in_dim.12), kind=kLoop, calls=%fused_computation | loop fusion | flops 20447232 | bytes 20447232 | tf_op jit(solution)/shard_map/concatenate | solution.py:58
  15.7 5.9 %all-to-all-start = ((bf16[8,128,4992]{2,1,0:T(8,128)(2,1)}), bf16[8,128,4992]{2,1,0:T(8,128)(2,1)}, u32[]{:S(2)}, u32[]{:S(2)}) async-start(bf16[8,128,4992]{2,1,0:T(8,128)(2,1)} %pad_maximum_fusion), calls=%async_computation | async-start | bytes 20447232 | tf_op jit(solution)/shard_map/all_to_all | solution.py:65
  21.6 139.0 %all-to-all-done = bf16[8,128,4992]{2,1,0:T(8,128)(2,1)} async-done(((bf16[8,128,4992]{2,1,0:T(8,128)(2,1)}), bf16[8,128,4992]{2,1,0:T(8,128)(2,1)}, u32[]{:S(2)}, u32[]{:S(2)}) %all-to-all-start) | async-done | bytes 10223648 | tf_op jit(solution)/shard_map/all_to_all | solution.py:65
  160.5 13.4 %convert_bitcast_fusion = bf16[128,8,896]{2,0,1:T(8,128)(2,1)S(1)} fusion(bf16[896,4096]{1,0:T(8,128)(2,1)} %param.8, bf16[8,128,4992]{2,1,0:T(8,128)(2,1)} %all-to-all-done), kind=kOutput, calls=%fused_computation.9 | convolution fusion | flops 7517110272 | bytes 17563648 | tf_op jit(solution)/shard_map/ptd,hd->tph/dot_general | solution.py:68
  174.0 0.7 fusion.33
  174.7 0.7 fusion.32
  175.4 0.7 fusion.31
  176.1 0.7 fusion.30
  176.8 0.7 fusion.29
  177.5 0.7 fusion.28
  178.2 0.7 fusion.27
  178.9 2.2 fusion.17
  181.1 0.2 copy.18
  181.3 0.1 reshape.73
  181.4 0.1 reduce-precision_convert_fusion.1
  181.5 0.1 pad_maximum_fusion.1
  181.6 0.1 copy.26
  181.7 5.0 %fusion.5 = f32[288,4096]{1,0:T(8,128)S(1)} fusion(bf16[8,128,4992]{2,1,0:T(8,128)(2,1)} %all-to-all-done, bf16[288,8,128]{2,1,0:T(8,128)(2,1)S(1)} %bitcast.135), kind=kOutput, calls=%fused_computation.6 | convolution fusion | flops 2415919104 | bytes 13697024 | tf_op jit(solution)/shard_map/mpt,ptd->md/dot_general | solution.py:79
  186.7 0.3 fusion.15
  187.0 0.3 copy.27
  187.3 1.7 constant_dynamic-slice_fusion.3
  188.9 0.1 copy.34
  189.0 5.3 %collective-permute-start.2 = (f32[8,3,32,128]{3,2,1,0:T(8,128)S(1)}, f32[8,3,32,128]{3,2,1,0:T(8,128)}, u32[]{:S(2)}, u32[]{:S(2)}) collective-permute-start(f32[8,3,32,128]{3,2,1,0:T(8,128)S(1)} %bitcast.136), channel_id=1, source_target_pairs={{0,24},{8,16},{16,8},{24,0},{32,56},{40,48},{48,40},{56,32},{64,88... | collective-permute-start | bytes 1179656 | tf_op jit(solution)/shard_map/ppermute | solution.py:36
  194.3 0.1 copy.35
  194.4 0.1 collective-permute-start.1
  194.5 0.8 copy.36
  195.3 0.4 collective-permute-start
  195.7 0.7 fusion.26
  196.4 3.6 %all-to-all-start.1 = ((bf16[8,128,1,896]{3,1,2,0:T(8,128)(2,1)}), bf16[8,128,1,896]{3,1,2,0:T(8,128)(2,1)S(1)}, u32[]{:S(2)}, u32[]{:S(2)}) async-start(bf16[8,128,1,896]{3,1,2,0:T(8,128)(2,1)} %fusion.26), calls=%async_computation.1 | async-start | bytes 3670016 | tf_op jit(solution)/shard_map/all_to_all | solution.py:13
  200.1 12.9 %collective-permute-done.2 = f32[8,3,32,128]{3,2,1,0:T(8,128)} collective-permute-done((f32[8,3,32,128]{3,2,1,0:T(8,128)S(1)}, f32[8,3,32,128]{3,2,1,0:T(8,128)}, u32[]{:S(2)}, u32[]{:S(2)}) %collective-permute-start.2) | collective-permute-done | bytes 393248 | tf_op jit(solution)/shard_map/ppermute | solution.py:36
  213.0 13.9 %collective-permute-done.1 = f32[8,3,32,128]{3,2,1,0:T(8,128)} collective-permute-done((f32[8,3,32,128]{3,2,1,0:T(8,128)S(1)}, f32[8,3,32,128]{3,2,1,0:T(8,128)}, u32[]{:S(2)}, u32[]{:S(2)}) %collective-permute-start.1) | collective-permute-done | bytes 393248 | tf_op jit(solution)/shard_map/ppermute | solution.py:36
  227.0 1.4 fusion.25
  228.5 5.7 %collective-permute-start.9 = (f32[3,32,128]{2,1,0:T(8,128)S(1)}, f32[3,32,128]{2,1,0:T(8,128)S(1)}, u32[]{:S(2)}, u32[]{:S(2)}) collective-permute-start(f32[3,32,128]{2,1,0:T(8,128)S(1)} %get-tuple-element.17), channel_id=1, source_target_pairs={{0,224},{8,232},{16,240},{24,248},{32,192},{40,200},{48,208},{56,2... | collective-permute-start | bytes 147464 | tf_op jit(solution)/shard_map/ppermute | solution.py:41
  234.2 0.5 collective-permute-start.8
  234.7 3.5 %collective-permute-start.7 = (f32[3,32,128]{2,1,0:T(8,128)S(1)}, f32[3,32,128]{2,1,0:T(8,128)S(1)}, u32[]{:S(2)}, u32[]{:S(2)}) collective-permute-start(f32[3,32,128]{2,1,0:T(8,128)S(1)} %get-tuple-element.19), channel_id=1, source_target_pairs={{0,160},{8,168},{16,176},{24,184},{32,128},{40,136},{48,144},{56,1... | collective-permute-start | bytes 147464 | tf_op jit(solution)/shard_map/ppermute | solution.py:41
  238.2 1.8 collective-permute-start.6
  240.0 1.6 collective-permute-start.5
  241.7 1.9 collective-permute-start.3
  243.6 1.8 collective-permute-done.6
  245.4 3.2 %collective-permute-done.4 = f32[3,32,128]{2,1,0:T(8,128)S(1)} collective-permute-done((f32[3,32,128]{2,1,0:T(8,128)S(1)}, f32[3,32,128]{2,1,0:T(8,128)S(1)}, u32[]{:S(2)}, u32[]{:S(2)}) %collective-permute-start.4) | collective-permute-done | bytes 49184 | tf_op jit(solution)/shard_map/ppermute | solution.py:41
  248.7 0.4 fusion.16
  249.1 1.0 copy.25
  250.1 1.0 fusion.20
  251.1 2.4 copy.17
  253.5 3.9 %copy.24 = bf16[128,7168]{1,0:T(8,128)(2,1)} copy(bf16[128,7168]{0,1:T(8,128)(2,1)} %bitcast.130) | data formatting | bytes 3670016
  (20 shorter events, 0.1 us)
Async XLA Ops:
  0.6 178.3 %copy-start = (bf16[3,32,896]{2,1,0:T(8,128)(2,1)S(1)}, bf16[3,32,896]{2,1,0:T(8,128)(2,1)}, u32[]{:S(2)}) copy-start(bf16[3,32,896]{2,1,0:T(8,128)(2,1)} %param.9) | copy-start | bytes 516100
  4.6 3.2 %copy-start.1 = (bf16[128,4096]{1,0:T(8,128)(2,1)S(1)}, bf16[128,4096]{1,0:T(8,128)(2,1)}, u32[]{:S(2)}) copy-start(bf16[128,4096]{1,0:T(8,128)(2,1)} %param.7) | copy-start | bytes 3145732
  15.7 144.8 %all-to-all-start = ((bf16[8,128,4992]{2,1,0:T(8,128)(2,1)}), bf16[8,128,4992]{2,1,0:T(8,128)(2,1)}, u32[]{:S(2)}, u32[]{:S(2)}) async-start(bf16[8,128,4992]{2,1,0:T(8,128)(2,1)} %pad_maximum_fusion), calls=%async_computation | async-start | bytes 20447232 | tf_op jit(solution)/shard_map/all_to_all | solution.py:65
  189.0 24.0 %collective-permute-start.2 = (f32[8,3,32,128]{3,2,1,0:T(8,128)S(1)}, f32[8,3,32,128]{3,2,1,0:T(8,128)}, u32[]{:S(2)}, u32[]{:S(2)}) collective-permute-start(f32[8,3,32,128]{3,2,1,0:T(8,128)S(1)} %bitcast.136), channel_id=1, source_target_pairs={{0,24},{8,16},{16,8},{24,0},{32,56},{40,48},{48,40},{56,32},{64,88... | collective-permute-start | bytes 1179656 | tf_op jit(solution)/shard_map/ppermute | solution.py:36
  194.4 32.6 %collective-permute-start.1 = (f32[8,3,32,128]{3,2,1,0:T(8,128)S(1)}, f32[8,3,32,128]{3,2,1,0:T(8,128)}, u32[]{:S(2)}, u32[]{:S(2)}) collective-permute-start(f32[8,3,32,128]{3,2,1,0:T(8,128)S(1)} %bitcast.137), channel_id=1, source_target_pairs={{0,16},{8,24},{16,0},{24,8},{32,48},{40,56},{48,32},{56,40},{64,80... | collective-permute-start | bytes 1179656 | tf_op jit(solution)/shard_map/ppermute | solution.py:36
  195.3 31.7 %collective-permute-start = (f32[8,3,32,128]{3,2,1,0:T(8,128)}, f32[8,3,32,128]{3,2,1,0:T(8,128)}, u32[]{:S(2)}, u32[]{:S(2)}) collective-permute-start(f32[8,3,32,128]{3,2,1,0:T(8,128)} %bitcast.126), channel_id=1, source_target_pairs={{0,8},{8,0},{16,24},{24,16},{32,40},{40,32},{48,56},{56,48},{64,72... | collective-permute-start | bytes 1179656 | tf_op jit(solution)/shard_map/ppermute | solution.py:36
  196.4 54.7 %all-to-all-start.1 = ((bf16[8,128,1,896]{3,1,2,0:T(8,128)(2,1)}), bf16[8,128,1,896]{3,1,2,0:T(8,128)(2,1)S(1)}, u32[]{:S(2)}, u32[]{:S(2)}) async-start(bf16[8,128,1,896]{3,1,2,0:T(8,128)(2,1)} %fusion.26), calls=%async_computation.1 | async-start | bytes 3670016 | tf_op jit(solution)/shard_map/all_to_all | solution.py:13
  200.0 48.6 %copy-start.4 = (f32[1,3,32,128]{3,2,1,0:T(8,128)S(1)}, f32[1,3,32,128]{3,2,1,0:T(8,128)}, u32[]{:S(2)}) copy-start(f32[1,3,32,128]{3,2,1,0:T(8,128)} %param.10) | copy-start | bytes 147460
  200.1 48.6 %copy-start.3 = (f32[1,3,32,128]{3,2,1,0:T(8,128)S(1)}, f32[1,3,32,128]{3,2,1,0:T(8,128)}, u32[]{:S(2)}) copy-start(f32[1,3,32,128]{3,2,1,0:T(8,128)} %param.11) | copy-start | bytes 147460
  228.5 13.2 %collective-permute-start.9 = (f32[3,32,128]{2,1,0:T(8,128)S(1)}, f32[3,32,128]{2,1,0:T(8,128)S(1)}, u32[]{:S(2)}, u32[]{:S(2)}) collective-permute-start(f32[3,32,128]{2,1,0:T(8,128)S(1)} %get-tuple-element.17), channel_id=1, source_target_pairs={{0,224},{8,232},{16,240},{24,248},{32,192},{40,200},{48,208},{56,2... | collective-permute-start | bytes 147464 | tf_op jit(solution)/shard_map/ppermute | solution.py:41
  234.2 7.5 %collective-permute-start.8 = (f32[3,32,128]{2,1,0:T(8,128)S(1)}, f32[3,32,128]{2,1,0:T(8,128)S(1)}, u32[]{:S(2)}, u32[]{:S(2)}) collective-permute-start(f32[3,32,128]{2,1,0:T(8,128)S(1)} %get-tuple-element.18), channel_id=1, source_target_pairs={{0,192},{8,200},{16,208},{24,216},{32,224},{40,232},{48,240},{56,2... | collective-permute-start | bytes 147464 | tf_op jit(solution)/shard_map/ppermute | solution.py:41
  234.7 8.8 %collective-permute-start.7 = (f32[3,32,128]{2,1,0:T(8,128)S(1)}, f32[3,32,128]{2,1,0:T(8,128)S(1)}, u32[]{:S(2)}, u32[]{:S(2)}) collective-permute-start(f32[3,32,128]{2,1,0:T(8,128)S(1)} %get-tuple-element.19), channel_id=1, source_target_pairs={{0,160},{8,168},{16,176},{24,184},{32,128},{40,136},{48,144},{56,1... | collective-permute-start | bytes 147464 | tf_op jit(solution)/shard_map/ppermute | solution.py:41
  238.2 7.2 %collective-permute-start.6 = (f32[3,32,128]{2,1,0:T(8,128)S(1)}, f32[3,32,128]{2,1,0:T(8,128)S(1)}, u32[]{:S(2)}, u32[]{:S(2)}) collective-permute-start(f32[3,32,128]{2,1,0:T(8,128)S(1)} %get-tuple-element.20), channel_id=1, source_target_pairs={{0,128},{8,136},{16,144},{24,152},{32,160},{40,168},{48,176},{56,1... | collective-permute-start | bytes 147464 | tf_op jit(solution)/shard_map/ppermute | solution.py:41
  240.0 5.4 %collective-permute-start.5 = (f32[3,32,128]{2,1,0:T(8,128)S(1)}, f32[3,32,128]{2,1,0:T(8,128)S(1)}, u32[]{:S(2)}, u32[]{:S(2)}) collective-permute-start(f32[3,32,128]{2,1,0:T(8,128)S(1)} %get-tuple-element.21), channel_id=1, source_target_pairs={{0,96},{8,104},{16,112},{24,120},{32,64},{40,72},{48,80},{56,88},{... | collective-permute-start | bytes 147464 | tf_op jit(solution)/shard_map/ppermute | solution.py:41
  241.6 7.0 %collective-permute-start.4 = (f32[3,32,128]{2,1,0:T(8,128)S(1)}, f32[3,32,128]{2,1,0:T(8,128)S(1)}, u32[]{:S(2)}, u32[]{:S(2)}) collective-permute-start(f32[3,32,128]{2,1,0:T(8,128)S(1)} %get-tuple-element.22), channel_id=1, source_target_pairs={{0,64},{8,72},{16,80},{24,88},{32,96},{40,104},{48,112},{56,120},{... | collective-permute-start | bytes 147464 | tf_op jit(solution)/shard_map/ppermute | solution.py:41
  241.7 7.0 %collective-permute-start.3 = (f32[3,32,128]{2,1,0:T(8,128)S(1)}, f32[3,32,128]{2,1,0:T(8,128)S(1)}, u32[]{:S(2)}, u32[]{:S(2)}) collective-permute-start(f32[3,32,128]{2,1,0:T(8,128)S(1)} %get-tuple-element.16), channel_id=1, source_target_pairs={{0,32},{8,40},{16,48},{24,56},{32,0},{40,8},{48,16},{56,24},{64,96... | collective-permute-start | bytes 147464 | tf_op jit(solution)/shard_map/ppermute | solution.py:41
  248.7 4.9 %copy-start.2 = (f32[1,3,32,128]{3,2,1,0:T(8,128)}, f32[1,3,32,128]{3,2,1,0:T(8,128)S(1)}, u32[]{:S(2)}) copy-start(f32[1,3,32,128]{3,2,1,0:T(8,128)S(1)} %bitcast_add_fusion.1) | copy-start | bytes 147460
